TPU v7x, 256 devices: a whole 4x4x8 slice. The times are simulated.
256 devices in a mesh: dom: 32 (over y_hi, z, core), tp: 8 (over x, y_lo).
Axes of the slice: x: 4, y: 4 (y_hi: 2, y_lo: 2; y = y_hi * 2 + y_lo), z: 8, core: 2. Of those that a mesh axis runs over, the one named last changes fastest.
Arguments:
- hidden_in: bfloat16 [448, 64, 4096], P('dom', None, 'tp'), may hold values from -6 to 6
- query_weight: bfloat16 [4096, 4096], P('dom', 'tp'), may hold values from -0.09375 to 0.09375
- segment_keys: bfloat16 [448, 64, 1024], P('dom', None, 'tp'), may hold values from -6 to 6
- segment_values: bfloat16 [448, 64, 1024], P('dom', None, 'tp'), may hold values from -6 to 6
- prefix_keys: bfloat16 [32, 256, 1024], P('dom', None, 'tp'), may hold values from -80 to 80
- prefix_values: bfloat16 [32, 256, 1024], P('dom', None, 'tp'), may hold values from -6 to 6
- ancestors: int32 [448], P('dom'), may hold values from 0 to 31, as said below
- twist_weights: float32 [448], P('dom'), may hold values from 0.25 to 4
- out_grad: bfloat16 [448, 64, 4096], P('dom', None, 'tp'), may hold values from -24 to 24
Outputs:
- grad_query_weight: bfloat16 [4096, 4096], P('dom', 'tp')
- grad_segment_keys: bfloat16 [448, 64, 1024], P('dom', None, 'tp')
- grad_segment_values: bfloat16 [448, 64, 1024], P('dom', None, 'tp')
- grad_prefix_keys: float32 [32, 256, 1024], P('dom', None, 'tp')
- grad_prefix_values: float32 [32, 256, 1024], P('dom', None, 'tp')
Inputs may be any that keep to these rules, and one draw needn't show every extreme that they name: `ancestors`: among the 14 consecutive particles of one device, no ancestor is named more than 2 times, and one ancestor, the same for all devices, is named exactly 2 times on every device.
All inputs are finite; a program needn't handle non-finite values.
Results may differ from a plain program's by a relative error of at most 0.02.
The roundings to bfloat16 on the way count: a program that leaves them out, or rounds other values in their place, can miss the bound.
Values may be sent and summed in bfloat16 or wider, within the bound.
No kernel may reach another device: no remote copies, remote signals or barrier semaphores. Data moves between devices by JAX's collectives and lax.ppermute only.
A program may use at most 128 MiB of HBM per device.

v0:
```python
import math
import jax
import jax.numpy as jnp
from jax import lax
from jax.sharding import PartitionSpec as P

HD = 128


def attend(queries, scaled, seg_keys, seg_values, pre_keys, pre_values):
    factor = 1.0 / math.sqrt(queries.shape[-1])
    score_pre = (
        jnp.einsum("bikgd,bjkd->bkgij", queries, pre_keys, preferred_element_type=jnp.float32)
        * factor
    )
    score_seg = (
        jnp.einsum("bikgd,bjkd->bkgij", queries, seg_keys, preferred_element_type=jnp.float32)
        * factor
    )
    length = queries.shape[1]
    causal = lax.broadcasted_iota(jnp.int32, (length, length), 0) >= lax.broadcasted_iota(
        jnp.int32, (length, length), 1
    )
    score_seg = jnp.where(causal, score_seg, -jnp.inf)
    row_max = jnp.maximum(jnp.max(score_pre, -1), jnp.max(score_seg, -1))[..., None]
    exp_pre = jnp.exp(score_pre - row_max)
    exp_seg = jnp.exp(score_seg - row_max)
    denominator = (jnp.sum(exp_pre, -1) + jnp.sum(exp_seg, -1))[..., None]
    prob_pre = exp_pre / denominator
    prob_seg = exp_seg / denominator
    dprob_pre = jnp.einsum(
        "bikgd,bjkd->bkgij", scaled, pre_values, preferred_element_type=jnp.float32
    )
    dprob_seg = jnp.einsum(
        "bikgd,bjkd->bkgij", scaled, seg_values, preferred_element_type=jnp.float32
    )
    row_delta = (jnp.sum(prob_pre * dprob_pre, -1) + jnp.sum(prob_seg * dprob_seg, -1))[..., None]
    dscore_pre = (prob_pre * (dprob_pre - row_delta)).astype(jnp.bfloat16)
    dscore_seg = (prob_seg * (dprob_seg - row_delta)).astype(jnp.bfloat16)
    grad_q = (
        jnp.einsum("bkgij,bjkd->bikgd", dscore_pre, pre_keys, preferred_element_type=jnp.float32)
        + jnp.einsum("bkgij,bjkd->bikgd", dscore_seg, seg_keys, preferred_element_type=jnp.float32)
    ) * factor
    grad_pk = (
        jnp.einsum("bkgij,bikgd->bjkd", dscore_pre, queries, preferred_element_type=jnp.float32)
        * factor
    )
    grad_pv = jnp.einsum(
        "bkgij,bikgd->bjkd",
        prob_pre.astype(jnp.bfloat16),
        scaled,
        preferred_element_type=jnp.float32,
    )
    grad_sk = (
        jnp.einsum("bkgij,bikgd->bjkd", dscore_seg, queries, preferred_element_type=jnp.float32)
        * factor
    )
    grad_sv = jnp.einsum(
        "bkgij,bikgd->bjkd",
        prob_seg.astype(jnp.bfloat16),
        scaled,
        preferred_element_type=jnp.float32,
    )
    return (
        grad_q.astype(jnp.bfloat16),
        grad_sk.astype(jnp.bfloat16),
        grad_sv.astype(jnp.bfloat16),
        grad_pk,
        grad_pv,
    )


def local(
    hidden_in,
    query_weight,
    segment_keys,
    segment_values,
    prefix_keys,
    prefix_values,
    ancestors,
    twist_weights,
    out_grad,
):
    particles_here = hidden_in.shape[0]
    length = hidden_in.shape[1]
    owners = lax.axis_size("dom")
    features = lax.all_gather(hidden_in, "tp", axis=2, tiled=True)
    token_rows = features.reshape(particles_here * length, features.shape[2])
    width_q = query_weight.shape[1]
    width_kv = segment_keys.shape[2]
    kv_heads = width_kv // HD
    group_size = width_q // width_kv
    prefix = prefix_keys.shape[1]
    queries = jnp.dot(
        token_rows,
        lax.all_gather(query_weight, "dom", axis=0, tiled=True),
        preferred_element_type=jnp.float32,
    ).astype(jnp.bfloat16)
    queries = queries.reshape(particles_here, length, width_q)
    scaled = (out_grad.astype(jnp.float32) * twist_weights[:, None, None]).astype(jnp.bfloat16)
    own_kv = jnp.concatenate([prefix_keys, prefix_values], axis=2)
    every_kv = lax.all_to_all(
        jnp.broadcast_to(own_kv, (owners,) + own_kv.shape[1:]),
        "dom",
        split_axis=0,
        concat_axis=0,
        tiled=True,
    )
    picked = jnp.take(every_kv, ancestors, axis=0)
    pre_keys = picked[:, :, :width_kv]
    pre_values = picked[:, :, width_kv:]
    grad_q, grad_sk, grad_sv, grad_pk, grad_pv = attend(
        queries.reshape(particles_here, length, kv_heads, group_size, HD),
        scaled.reshape(particles_here, length, kv_heads, group_size, HD),
        segment_keys.reshape(particles_here, length, kv_heads, HD),
        segment_values.reshape(particles_here, length, kv_heads, HD),
        pre_keys.reshape(particles_here, prefix, kv_heads, HD),
        pre_values.reshape(particles_here, prefix, kv_heads, HD),
    )
    grad_pkv = jnp.concatenate(
        [
            grad_pk.reshape(particles_here, prefix, width_kv),
            grad_pv.reshape(particles_here, prefix, width_kv),
        ],
        axis=2,
    )
    owner_ids = jnp.arange(owners, dtype=jnp.int32)
    onehot = (owner_ids[:, None] == ancestors[None, :]).astype(jnp.float32)
    outgoing = jnp.einsum("ap,pjc->ajc", onehot, grad_pkv, precision=lax.Precision.HIGHEST)
    incoming = lax.all_to_all(outgoing, "dom", split_axis=0, concat_axis=0, tiled=True)
    summed = jnp.sum(incoming, axis=0)
    grad_pre_keys = summed[None, :, :width_kv]
    grad_pre_values = summed[None, :, width_kv:]
    grad_seg_keys = grad_sk.reshape(particles_here, length, width_kv)
    grad_seg_values = grad_sv.reshape(particles_here, length, width_kv)
    grad_rows = grad_q.reshape(particles_here * length, width_q)
    grad_weight = lax.psum_scatter(
        jnp.einsum("tc,tq->cq", token_rows, grad_rows, preferred_element_type=jnp.float32).astype(
            jnp.bfloat16
        ),
        "dom",
        scatter_dimension=0,
        tiled=True,
    )
    return (grad_weight, grad_seg_keys, grad_seg_values, grad_pre_keys, grad_pre_values)


def solution(mesh):
    return jax.shard_map(
        local,
        mesh=mesh,
        in_specs=(
            P("dom", None, "tp"),
            P("dom", "tp"),
            P("dom", None, "tp"),
            P("dom", None, "tp"),
            P("dom", None, "tp"),
            P("dom", None, "tp"),
            P("dom"),
            P("dom"),
            P("dom", None, "tp"),
        ),
        out_specs=(
            P("dom", "tp"),
            P("dom", None, "tp"),
            P("dom", None, "tp"),
            P("dom", None, "tp"),
            P("dom", None, "tp"),
        ),
        check_vma=False,
    )
```

profile of v0, /device:TPU:6, one launch (start us, length us, event | category | flops | bytes accessed | tf_op | source)
XLA Modules:
  0.0 559.1 jit_solution(17985210257255980945)
XLA Ops:
  7.2 0.0 copy-start
  7.2 0.0 all-gather.5.cloned.1.call-start
  7.2 0.7 all-gather.5.cloned.1.call-update
  7.9 0.0 all-gather.3.cloned.1.call-start
  8.0 0.7 all-gather.3.cloned.1.call-update
  8.7 0.9 maximum_bitcast_fusion
  9.6 2.4 broadcast_in_dim.41
  12.0 11.7 %all-to-all-start = ((bf16[32,256,256]{2,1,0:T(8,128)(2,1)}), bf16[32,256,256]{2,1,0:T(8,128)(2,1)}, u32[]{:S(2)}, u32[]{:S(2)}) async-start(bf16[32,256,256]{2,1,0:T(8,128)(2,1)} %broadcast_in_dim.41), calls=%async_computation | async-start | bytes 8388608 | tf_op jit(solution)/shard_map/all_to_all | solution.py:102
  23.8 111.2 %all-to-all-done = bf16[32,256,256]{2,1,0:T(8,128)(2,1)} async-done(((bf16[32,256,256]{2,1,0:T(8,128)(2,1)}), bf16[32,256,256]{2,1,0:T(8,128)(2,1)}, u32[]{:S(2)}, u32[]{:S(2)}) %all-to-all-start) | async-done | bytes 4194336 | tf_op jit(solution)/shard_map/all_to_all | solution.py:102
  135.0 4.2 gather_fusion
  139.2 1.7 broadcast_select_fusion
  140.9 0.0 all-gather.5.cloned.1.call-done
  140.9 145.1 %all-gather.3.cloned.1.call-done = bf16[14,64,4096]{2,1,0:T(8,128)(2,1)} async-done(((bf16[14,64,512]{2,1,0:T(8,128)(2,1)}), bf16[14,64,4096]{2,1,0:T(8,128)(2,1)}) %all-gather.3.cloned.1.call-update) | async-done | bytes 7340048 | tf_op jit(solution)/shard_map/all_gather | solution.py:87
  286.0 9.2 %convolution_convert_fusion.1 = bf16[896,512]{1,0:T(8,128)(2,1)} fusion(bf16[896,4096]{1,0:T(8,128)(2,1)} %bitcast.207, bf16[4096,512]{1,0:T(8,128)(2,1)} %all-gather.5.cloned.1.call-done), kind=kOutput, calls=%fused_computation.35 | convolution fusion | flops 3758555136 | bytes 12451840 | tf_op jit(solution)/shard_map/dot_general | solution.py:94
  295.2 1.9 reshape.161
  297.0 0.7 bitcast_reduce_fusion
  297.8 1.0 fusion.60
  298.9 1.2 fusion.6
  300.1 0.0 copy-start.8
  300.1 0.4 fusion.19
  300.6 0.7 copy-done.8
  301.3 2.6 fusion.1
  303.9 2.9 fusion.20
  306.9 2.4 fusion.13
  309.3 1.8 fusion.7
  311.1 0.5 fusion.10
  311.6 2.2 pad_maximum_fusion
  313.7 5.4 copy.47
  319.1 5.7 %fusion.55 = f32[32,256,256]{2,0,1:T(8,128)S(1)} fusion(f32[14,256,256]{2,0,1:T(8,128)} %copy.47, s32[14]{0:T(128)S(1)} %copy-done.7), kind=kOutput, calls=%fused_computation.77 | convolution fusion | flops 352321984 | bytes 12058680 | tf_op jit(solution)/shard_map/ap,pjc->ajc/dot_general | solution.py:129
  324.8 8.1 %copy.48 = f32[32,256,256]{2,1,0:T(8,128)} copy(f32[32,256,256]{2,0,1:T(8,128)S(1)} %fusion.55) | data formatting | bytes 16777216 | tf_op jit(solution)/shard_map/ap,pjc->ajc/dot_general | solution.py:129
  332.9 13.0 %all-to-all-start.1 = ((f32[32,256,256]{2,1,0:T(8,128)}), f32[32,256,256]{2,1,0:T(8,128)}, u32[]{:S(2)}, u32[]{:S(2)}) async-start(f32[32,256,256]{2,1,0:T(8,128)} %copy.48), calls=%async_computation.1 | async-start | bytes 16777216 | tf_op jit(solution)/shard_map/all_to_all | solution.py:130
  345.9 0.0 reduce-scatter.4.cloned.1.call-start
  345.9 2.7 fusion.30
  348.6 0.9 copy-done.5
  349.6 0.5 fusion.51
  350.0 1.0 copy-done.4
  351.1 0.7 fusion.23
  351.7 0.8 copy.42
  352.5 9.5 %fusion = bf16[4096,512]{0,1:T(8,128)(2,1)} fusion(bf16[896,4096]{1,0:T(8,128)(2,1)} %bitcast.208, bf16[112,8,4,128]{3,2,1,0:T(4,128)(2,1)S(1)} %bitcast.206), kind=kOutput, calls=%fused_computation.2 | convolution fusion | flops 3760193536 | bytes 12451840 | tf_op jit(solution)/shard_map/tc,tq->cq/dot_general | solution.py:138
  362.0 6.5 %copy.59 = bf16[4096,512]{1,0:T(8,128)(2,1)} copy(bf16[4096,512]{0,1:T(8,128)(2,1)} %fusion) | data formatting | bytes 8388608
  368.5 0.0 reduce-scatter.4.cloned.1.call-update
  368.5 1.2 copy-done.6
  369.6 1.1 fusion.27
  370.7 0.6 copy-done.2
  371.3 1.3 fusion.28
  372.6 175.3 %all-to-all-done.1 = f32[32,256,256]{2,1,0:T(8,128)} async-done(((f32[32,256,256]{2,1,0:T(8,128)}), f32[32,256,256]{2,1,0:T(8,128)}, u32[]{:S(2)}, u32[]{:S(2)}) %all-to-all-start.1) | async-done | bytes 8388640 | tf_op jit(solution)/shard_map/all_to_all | solution.py:130
  547.9 3.9 reduce_sum.49
  551.8 0.7 slice_bitcast_fusion.5
  (25 shorter events, 0.1 us)
Async XLA Ops:
  7.2 290.6 %copy-start = (bf16[14,64,128]{2,1,0:T(8,128)(2,1)S(1)}, bf16[14,64,128]{2,1,0:T(8,128)(2,1)}, u32[]{:S(2)}) copy-start(bf16[14,64,128]{2,1,0:T(8,128)(2,1)} %param.11) | copy-start | bytes 688132
  7.2 133.8 %all-gather.5.cloned.1.call-start = ((), (), s32[]{:S(2)}) async-start(), calls=%async_computation.4 | async-start | bytes 4325376 | tf_op jit(solution)/shard_map/all_gather | solution.py:96
  7.9 278.1 %all-gather.3.cloned.1.call-start = ((), (), s32[]{:S(2)}) async-start(), calls=%async_computation.3 | async-start | bytes 8257536 | tf_op jit(solution)/shard_map/all_gather | solution.py:87
  12.0 11.8 %copy-start.7 = (s32[14]{0:T(128)S(1)}, s32[14]{0:T(128)}, u32[]{:S(2)}) copy-start(s32[14]{0:T(128)} %param.15) | copy-start | bytes 172
  12.0 123.0 %all-to-all-start = ((bf16[32,256,256]{2,1,0:T(8,128)(2,1)}), bf16[32,256,256]{2,1,0:T(8,128)(2,1)}, u32[]{:S(2)}, u32[]{:S(2)}) async-start(bf16[32,256,256]{2,1,0:T(8,128)(2,1)} %broadcast_in_dim.41), calls=%async_computation | async-start | bytes 8388608 | tf_op jit(solution)/shard_map/all_to_all | solution.py:102
  140.9 159.7 %copy-start.3 = (bf16[14,256,256]{2,1,0:T(8,128)(2,1)}, bf16[14,256,256]{2,1,0:T(8,128)(2,1)S(1)}, u32[]{:S(2)}) copy-start(bf16[14,256,256]{2,1,0:T(8,128)(2,1)S(1)} %broadcast_select_fusion) | copy-start | bytes 5505028
  298.8 8.1 %copy-start.1 = (f32[14,1,4,64,64]{3,4,2,0,1:T(8,128)}, f32[14,1,4,64,64]{3,4,2,0,1:T(8,128)S(1)}, u32[]{:S(2)}) copy-start(f32[14,1,4,64,64]{3,4,2,0,1:T(8,128)S(1)} %get-tuple-element.25) | copy-start | bytes 2752516
  300.1 1.2 copy-start.8
  300.1 1.2 copy-start.11
  303.9 3.0 copy-start.10
  332.9 215.0 %all-to-all-start.1 = ((f32[32,256,256]{2,1,0:T(8,128)}), f32[32,256,256]{2,1,0:T(8,128)}, u32[]{:S(2)}, u32[]{:S(2)}) async-start(f32[32,256,256]{2,1,0:T(8,128)} %copy.48), calls=%async_computation.1 | async-start | bytes 16777216 | tf_op jit(solution)/shard_map/all_to_all | solution.py:130
  345.9 206.6 %reduce-scatter.4.cloned.1.call-start = ((), (), s32[]{:S(2)}) async-start(), calls=%async_computation.5 | async-start | bytes 4325376
  348.6 0.9 copy-start.5
  349.6 1.5 copy-start.4
  368.5 1.2 copy-start.6
  368.5 2.3 copy-start.9
  369.6 1.7 copy-start.2
Sparse Core Ops, SparseCore 0:
  10.8 122.8 all-gather.4
  135.5 150.5 all-gather.2
  368.6 177.9 reduce-scatter.3
where the time goes:
time: 560 us; the launch traced here: 559 us
  waiting for transfers between devices  433 us (77%)
  matrix products  38 us (7%)
  local copies, waits for them, and re-layouts  34.3 us (6%)
  starting transfers between devices  24.9 us (4%)
  other arithmetic  14.9 us (3%)
  between operations  14 us (2%)
    all_to_all x1, waiting for transfers between devices, local(): lax.all_to_all(outgoing, 'dom', split_axis=0, concat_axis=0, tiled=True)  175 us
    all_gather x1, waiting for transfers between devices, local(): features = lax.all_gather(hidden_in, 'tp', axis=2, tiled=True)  145 us
    all_to_all x1, waiting for transfers between devices, local(): lax.all_to_all(jnp.broadcast_to(own_kv, (owners,) + own_kv.shape[1:]), 'd...  111 us
    all_to_all x1, starting transfers between devices, local(): lax.all_to_all(outgoing, 'dom', split_axis=0, concat_axis=0, tiled=True)  13 us
    all_to_all x1, starting transfers between devices, local(): lax.all_to_all(jnp.broadcast_to(own_kv, (owners,) + own_kv.shape[1:]), 'd...  11.7 us
  transfers between devices with their start and end apart: 5, of which 3 were waited for; matrix products, arithmetic and copies ran while one was open for 7% of the time, Pallas kernels for 0%

commit v1 on v0

--- a/solution.py
+++ b/solution.py
@@ -84,7 +84,9 @@
     particles_here = hidden_in.shape[0]
     length = hidden_in.shape[1]
     owners = lax.axis_size("dom")
-    features = lax.all_gather(hidden_in, "tp", axis=2, tiled=True)
+    features = jnp.concatenate(
+        lax.all_to_all(jnp.stack([hidden_in] * lax.axis_size("tp")), "tp", 0, 0), axis=2
+    )
     token_rows = features.reshape(particles_here * length, features.shape[2])
     width_q = query_weight.shape[1]
     width_kv = segment_keys.shape[2]

time: 560 us -> 490 us (0.88)
  waiting for transfers between devices: 433 us -> 349 us
  local copies, waits for them, and re-layouts: 34.3 us -> 51.5 us
    all_gather x1 -> x0, waiting for transfers between devices: 145 us -> none  [local(): features = lax.all_gather(hidden_in, 'tp', axis=2, tiled=True)]
    all_to_all x0 -> x1, waiting for transfers between devices: none -> 98.4 us  [local(): lax.all_to_all(jnp.stack([hidden_in] * lax.axis_size('tp')), 'tp', 0, 0)]
    all_to_all x1, waiting for transfers between devices: 111 us -> 72 us  [local(): lax.all_to_all(jnp.broadcast_to(own_kv, (owners,) + own_kv.shape[1:]), 'd...]
    reshape x0 -> x1, local copies, waits for them, and re-layouts: none -> 8.14 us  [local(): jnp.concatenate(lax.all_to_all(jnp.stack([hidden_in] * lax.axis_size('tp'...]
    all_to_all x0 -> x1, starting transfers between devices: none -> 7.07 us  [local(): lax.all_to_all(jnp.stack([hidden_in] * lax.axis_size('tp')), 'tp', 0, 0)]
    unnamed x25 -> x34, local copies, waits for them, and re-layouts: 10.9 us -> 17.7 us
    all_to_all x1, starting transfers between devices: 13 us -> 6.66 us  [local(): lax.all_to_all(outgoing, 'dom', split_axis=0, concat_axis=0, tiled=True)]
  transfers between devices with their start and end apart: 5 -> 5, of which waited for: 3 -> 3; matrix products, arithmetic and copies ran while one was open for 7% -> 11% of each run, Pallas kernels for 0% -> 0%
where the time goes in v1:
time: 490 us; the launch traced here: 488 us
  waiting for transfers between devices  349 us (71%)
  local copies, waits for them, and re-layouts  51.5 us (11%)
  matrix products  34.4 us (7%)
  starting transfers between devices  25.2 us (5%)
  between operations  14.4 us (3%)
  other arithmetic  12.7 us (3%)
    all_to_all x1, waiting for transfers between devices, local(): lax.all_to_all(outgoing, 'dom', split_axis=0, concat_axis=0, tiled=True)  178 us
    all_to_all x1, waiting for transfers between devices, local(): lax.all_to_all(jnp.stack([hidden_in] * lax.axis_size('tp')), 'tp', 0, 0)  98.4 us
    all_to_all x1, waiting for transfers between devices, local(): lax.all_to_all(jnp.broadcast_to(own_kv, (owners,) + own_kv.shape[1:]), 'd...  72 us
    unnamed x34, local copies, waits for them, and re-layouts  17.7 us
    all_to_all x1, starting transfers between devices, local(): lax.all_to_all(jnp.broadcast_to(own_kv, (owners,) + own_kv.shape[1:]), 'd...  11.4 us
  transfers between devices with their start and end apart: 5, of which 3 were waited for; matrix products, arithmetic and copies ran while one was open for 11% of the time, Pallas kernels for 0%

profile of v1, /device:TPU:6, one launch (start us, length us, event | category | flops | bytes accessed | tf_op | source)
XLA Modules:
  0.0 487.7 jit_solution(4773126330402772522)
XLA Ops:
  7.2 0.0 copy-start
  7.2 5.2 %stack.2 = bf16[8,14,64,512]{3,2,1,0:T(8,128)(2,1)} broadcast(bf16[14,64,512]{2,1,0:T(8,128)(2,1)} %param.9), dimensions={1,2,3} | broadcast | bytes 8257536 | tf_op jit(solution)/shard_map/stack | solution.py:88
  12.3 7.1 %all-to-all-start.1 = ((bf16[8,14,64,512]{3,2,1,0:T(8,128)(2,1)}), bf16[8,14,64,512]{3,2,1,0:T(8,128)(2,1)}, u32[]{:S(2)}, u32[]{:S(2)}) async-start(bf16[8,14,64,512]{3,2,1,0:T(8,128)(2,1)} %stack.2), calls=%async_computation.1 | async-start | bytes 14680064 | tf_op jit(solution)/shard_map/all_to_all | solution.py:88
  19.4 0.7 all-gather.2.cloned.1.call-update
  20.2 98.4 %all-to-all-done.1 = bf16[8,14,64,512]{3,2,1,0:T(8,128)(2,1)} async-done(((bf16[8,14,64,512]{3,2,1,0:T(8,128)(2,1)}), bf16[8,14,64,512]{3,2,1,0:T(8,128)(2,1)}, u32[]{:S(2)}, u32[]{:S(2)}) %all-to-all-start.1) | async-done | bytes 7340064 | tf_op jit(solution)/shard_map/all_to_all | solution.py:88
  118.6 2.5 broadcast_in_dim.41
  121.1 11.4 %all-to-all-start = ((bf16[32,256,256]{2,1,0:T(8,128)(2,1)}), bf16[32,256,256]{2,1,0:T(8,128)(2,1)}, u32[]{:S(2)}, u32[]{:S(2)}) async-start(bf16[32,256,256]{2,1,0:T(8,128)(2,1)} %broadcast_in_dim.41), calls=%async_computation | async-start | bytes 8388608 | tf_op jit(solution)/shard_map/all_to_all | solution.py:104
  132.6 8.1 %copy.37 = bf16[14,64,8,512]{3,2,1,0:T(8,128)(2,1)S(1)} copy(bf16[14,64,8,512]{3,1,0,2:T(8,128)(2,1)} %bitcast.4) | data formatting | bytes 14680064 | tf_op jit(solution)/shard_map/reshape | solution.py:87
  140.7 7.8 %copy.63 = bf16[112,8,8,512]{3,1,2,0:T(8,128)(2,1)} copy(bf16[112,8,8,512]{3,2,1,0:T(8,128)(2,1)S(1)} %bitcast.209) | data formatting | bytes 14680064
  148.6 8.4 %convolution_convert_fusion.1 = bf16[896,512]{1,0:T(8,128)(2,1)S(1)} fusion(bf16[896,4096]{1,0:T(8,128)(2,1)} %bitcast.210, bf16[4096,512]{1,0:T(8,128)(2,1)} %all-gather.2.cloned.1.call-done), kind=kOutput, calls=%fused_computation.35 | convolution fusion | flops 3758555136 | bytes 12451840 | tf_op jit(solution)/shard_map/dot_general | solution.py:96
  157.0 0.2 reshape.163
  157.2 72.0 %all-to-all-done = bf16[32,256,256]{2,1,0:T(8,128)(2,1)} async-done(((bf16[32,256,256]{2,1,0:T(8,128)(2,1)}), bf16[32,256,256]{2,1,0:T(8,128)(2,1)}, u32[]{:S(2)}, u32[]{:S(2)}) %all-to-all-start) | async-done | bytes 4194336 | tf_op jit(solution)/shard_map/all_to_all | solution.py:104
  229.2 2.9 gather_fusion
  232.1 0.2 broadcast_select_fusion
  232.3 0.7 bitcast_reduce_fusion
  233.1 1.0 fusion.60
  234.1 1.2 fusion.6
  235.4 0.0 copy-start.10
  235.4 0.0 copy-start.13
  235.4 0.4 fusion.19
  235.8 0.7 copy-done.10
  236.5 2.6 fusion.1
  239.2 0.0 copy-start.12
  239.2 2.9 fusion.20
  242.2 2.4 fusion.13
  244.6 1.8 fusion.7
  246.4 0.5 fusion.10
  246.9 2.2 pad_maximum_fusion
  249.0 5.4 %copy.48 = f32[14,256,256]{2,0,1:T(8,128)} copy(f32[14,256,256]{1,2,0:T(8,128)} %pad_maximum_fusion) | data formatting | bytes 7340032 | tf_op jit(solution)/shard_map/concatenate | solution.py:122
  254.4 5.7 %fusion.55 = f32[32,256,256]{2,0,1:T(8,128)S(1)} fusion(f32[14,256,256]{2,0,1:T(8,128)} %copy.48, s32[14]{0:T(128)S(1)} %copy-done.9), kind=kOutput, calls=%fused_computation.77 | convolution fusion | flops 352321984 | bytes 12058680 | tf_op jit(solution)/shard_map/ap,pjc->ajc/dot_general | solution.py:131
  260.2 8.1 %copy.49 = f32[32,256,256]{2,1,0:T(8,128)} copy(f32[32,256,256]{2,0,1:T(8,128)S(1)} %fusion.55) | data formatting | bytes 16777216 | tf_op jit(solution)/shard_map/ap,pjc->ajc/dot_general | solution.py:131
  268.3 6.7 %all-to-all-start.2 = ((f32[32,256,256]{2,1,0:T(8,128)}), f32[32,256,256]{2,1,0:T(8,128)}, u32[]{:S(2)}, u32[]{:S(2)}) async-start(f32[32,256,256]{2,1,0:T(8,128)} %copy.49), calls=%async_computation.2 | async-start | bytes 16777216 | tf_op jit(solution)/shard_map/all_to_all | solution.py:132
  274.9 0.0 reduce-scatter.4.cloned.1.call-start
  275.0 2.8 fusion.30
  277.8 1.0 copy-done.5
  278.8 0.5 fusion.51
  279.3 0.7 fusion.23
  279.9 0.8 copy.43
  280.7 6.5 %fusion = bf16[4096,512]{0,1:T(8,128)(2,1)} fusion(bf16[896,4096]{1,0:T(8,128)(2,1)S(1)} %bitcast.213, bf16[112,8,4,128]{3,2,1,0:T(4,128)(2,1)S(1)} %bitcast.214), kind=kOutput, calls=%fused_computation.2 | convolution fusion | flops 3760193536 | bytes 12451840 | tf_op jit(solution)/shard_map/tc,tq->cq/dot_general | solution.py:140
  287.2 6.5 %copy.60 = bf16[4096,512]{1,0:T(8,128)(2,1)} copy(bf16[4096,512]{0,1:T(8,128)(2,1)} %fusion) | data formatting | bytes 8388608
  293.7 0.0 reduce-scatter.4.cloned.1.call-update
  293.7 1.2 copy-done.6
  294.9 1.1 fusion.27
  296.0 0.6 copy-done.2
  296.5 1.3 fusion.28
  297.9 178.4 %all-to-all-done.2 = f32[32,256,256]{2,1,0:T(8,128)} async-done(((f32[32,256,256]{2,1,0:T(8,128)}), f32[32,256,256]{2,1,0:T(8,128)}, u32[]{:S(2)}, u32[]{:S(2)}) %all-to-all-start.2) | async-done | bytes 8388640 | tf_op jit(solution)/shard_map/all_to_all | solution.py:132
  476.2 3.9 reduce_sum.49
  480.2 0.7 slice_bitcast_fusion.5
  (36 shorter events, 0.1 us)
Async XLA Ops:
  7.2 225.9 %copy-start = (bf16[14,64,128]{2,1,0:T(8,128)(2,1)S(1)}, bf16[14,64,128]{2,1,0:T(8,128)(2,1)}, u32[]{:S(2)}) copy-start(bf16[14,64,128]{2,1,0:T(8,128)(2,1)} %param.11) | copy-start | bytes 688132
  12.3 7.8 %copy-start.7 = (bf16[1,256,128]{2,1,0:T(8,128)(2,1)S(1)}, bf16[1,256,128]{2,1,0:T(8,128)(2,1)}, u32[]{:S(2)}) copy-start(bf16[1,256,128]{2,1,0:T(8,128)(2,1)} %param.14) | copy-start | bytes 196612
  12.3 7.8 %copy-start.8 = (bf16[1,256,128]{2,1,0:T(8,128)(2,1)S(1)}, bf16[1,256,128]{2,1,0:T(8,128)(2,1)}, u32[]{:S(2)}) copy-start(bf16[1,256,128]{2,1,0:T(8,128)(2,1)} %param.13) | copy-start | bytes 196612
  12.3 106.2 %all-to-all-start.1 = ((bf16[8,14,64,512]{3,2,1,0:T(8,128)(2,1)}), bf16[8,14,64,512]{3,2,1,0:T(8,128)(2,1)}, u32[]{:S(2)}, u32[]{:S(2)}) async-start(bf16[8,14,64,512]{3,2,1,0:T(8,128)(2,1)} %stack.2), calls=%async_computation.1 | async-start | bytes 14680064 | tf_op jit(solution)/shard_map/all_to_all | solution.py:88
  19.4 129.1 %all-gather.2.cloned.1.call-start = ((), (), s32[]{:S(2)}) async-start(), calls=%async_computation.4 | async-start | bytes 4325376 | tf_op jit(solution)/shard_map/all_gather | solution.py:98
  121.1 11.5 %copy-start.9 = (s32[14]{0:T(128)S(1)}, s32[14]{0:T(128)}, u32[]{:S(2)}) copy-start(s32[14]{0:T(128)} %param.15) | copy-start | bytes 172
  121.1 108.1 %all-to-all-start = ((bf16[32,256,256]{2,1,0:T(8,128)(2,1)}), bf16[32,256,256]{2,1,0:T(8,128)(2,1)}, u32[]{:S(2)}, u32[]{:S(2)}) async-start(bf16[32,256,256]{2,1,0:T(8,128)(2,1)} %broadcast_in_dim.41), calls=%async_computation | async-start | bytes 8388608 | tf_op jit(solution)/shard_map/all_to_all | solution.py:104
  232.3 3.5 copy-start.3
  234.1 8.1 %copy-start.1 = (f32[14,1,4,64,64]{3,4,2,0,1:T(8,128)}, f32[14,1,4,64,64]{3,4,2,0,1:T(8,128)S(1)}, u32[]{:S(2)}) copy-start(f32[14,1,4,64,64]{3,4,2,0,1:T(8,128)S(1)} %get-tuple-element.25) | copy-start | bytes 2752516
  235.4 1.2 copy-start.10
  235.4 1.2 copy-start.13
  239.2 3.0 copy-start.12
  268.3 208.0 %all-to-all-start.2 = ((f32[32,256,256]{2,1,0:T(8,128)}), f32[32,256,256]{2,1,0:T(8,128)}, u32[]{:S(2)}, u32[]{:S(2)}) async-start(f32[32,256,256]{2,1,0:T(8,128)} %copy.49), calls=%async_computation.2 | async-start | bytes 16777216 | tf_op jit(solution)/shard_map/all_to_all | solution.py:132
  274.9 206.0 %reduce-scatter.4.cloned.1.call-start = ((), (), s32[]{:S(2)}) async-start(), calls=%async_computation.5 | async-start | bytes 4325376
  275.0 4.3 copy-start.4
  275.0 5.7 %slice-start = ((s8[7340032]{0:T(1024)(128)(4,1)}), s8[4194304]{0:T(1024)(128)(4,1)S(1)}, s32[]{:S(2)}) async-start(s8[7340032]{0:T(1024)(128)(4,1)} %bitcast.211), calls=%async_computation.6 | async-start | bytes 8388608
  277.8 1.0 copy-start.5
  278.8 1.9 slice-start.1
  293.7 1.2 copy-start.6
  293.7 2.3 copy-start.11
  294.9 1.7 copy-start.2
Sparse Core Ops, SparseCore 0:
  23.0 114.5 all-gather.1
  293.9 186.6 reduce-scatter.3
